TPU v7x, 512 devices: a whole 4x4x16 slice. The times are simulated.
512 devices in a mesh: blk: 32 (over z, core), col: 16 (over y, x).
Axes of the slice: x: 4, y: 4, z: 16, core: 2. Of those that a mesh axis runs over, the one named last changes fastest.
Arguments:
- density: float32 [96, 7, 256, 256], P('blk', None, 'col'), as said below
- band_widths: int32 [96], P('blk'), may hold values from 1 to 3, as said below
Outputs:
- purified: float32 [96, 7, 256, 256], P('blk', None, 'col')
Inputs may be any that keep to these rules, and one draw needn't show every extreme that they name: `band_widths`: each block row keeps between 1 and 3 blocks on each side; 3 is reached in every draw. `density`: diagonal entries of the diagonal blocks lie between 0.05 and 0.95, all other entries are small.
All inputs are finite; a program needn't handle non-finite values.
Results may differ from a plain program's by a relative error of at most 0.00013.
Values sent between devices are 32-bit elements; how exact they have to be, the bound alone decides.
No kernel may reach another device: no remote copies, remote signals or barrier semaphores. Data moves between devices by JAX's collectives and lax.ppermute only.
A program may use at most 64 MiB of HBM per device.

v0:
```python
import jax
import jax.numpy as jnp
from jax import lax
from jax.sharding import PartitionSpec as P

W = 3


def padded(cells, sides, width):
    for axis, dim in sides:
        count = lax.axis_size(axis)
        head = lax.slice_in_dim(cells, 0, width, axis=dim)
        tail = lax.slice_in_dim(cells, cells.shape[dim] - width, cells.shape[dim], axis=dim)
        cells = jnp.concatenate(
            [
                lax.ppermute(tail, axis, [(i, (i + 1) % count) for i in range(count)]),
                cells,
                lax.ppermute(head, axis, [((i + 1) % count, i) for i in range(count)]),
            ],
            axis=dim,
        )
    return cells


def extend(right):
    return padded(right, (("blk", 0),), W)


def contract(extended, shard_rows):
    local_rows = shard_rows.shape[0]
    summed_bands = [None] * (2 * W + 1)
    for inner_band in range(2 * W + 1):
        lowest = max(0, inner_band - W)
        highest = min(2 * W, inner_band + W)
        source_low = lowest - inner_band + W
        source_high = highest - inner_band + W
        block_terms = jnp.einsum(
            "ibcs,isr->ibcr",
            extended[inner_band : inner_band + local_rows, source_low : source_high + 1],
            shard_rows[:, inner_band],
            precision=lax.Precision.HIGHEST,
        )
        for right_band in range(lowest, highest + 1):
            term = block_terms[:, right_band - lowest]
            summed_bands[right_band] = (
                term if summed_bands[right_band] is None else summed_bands[right_band] + term
            )
    return jnp.stack(summed_bands, axis=1)


def on_device(density, band_widths):
    offsets = jnp.abs(jnp.arange(2 * W + 1, dtype=jnp.int32) - W)
    pattern = (offsets[None, :] <= band_widths[:, None]).astype(jnp.float32)[:, :, None, None]
    current = density * pattern
    for purify_step in range(2):
        gathered = lax.all_gather(current, "col", axis=2, tiled=True)
        square = contract(extend(current), gathered) * pattern
        third_power = contract(extend(square), gathered) * pattern
        current = 3.0 * square - 2.0 * third_power
    return current


def solution(mesh):
    in_specs = (P("blk", None, "col", None), P("blk"))
    out_specs = P("blk", None, "col", None)
    return jax.shard_map(
        on_device, mesh=mesh, in_specs=in_specs, out_specs=out_specs, check_vma=False
    )
```

profile of v0, /device:TPU:2, one launch (start us, length us, event | category | flops | bytes accessed | tf_op | source)
XLA Modules:
  0.0 212.1 jit_solution(5076322240943868647)
XLA Ops:
  6.5 0.0 all-gather.3.cloned.1.call-start
  6.5 0.7 compare_convert_fusion
  7.3 1.8 copy_multiply_fusion
  9.1 0.0 copy-start.2
  9.1 0.0 all-gather.3.cloned.1.call-update
  9.1 0.0 all-gather.5.cloned.1.call-start
  9.1 0.0 collective-permute-start
  9.2 8.9 %collective-permute-start.1 = (f32[3,7,16,256]{3,2,0,1:T(8,128)}, f32[3,7,16,256]{3,2,0,1:T(8,128)S(1)}, u32[]{:S(2)}, u32[]{:S(2)}) collective-permute-start(f32[3,7,16,256]{3,2,0,1:T(8,128)} %copy_multiply_fusion), channel_id=1, source_target_pairs={{16,0},{32,16},{48,32},{64,48},{80,64},{96,80},{112,96},{128,112},... | collective-permute-start | bytes 1032200 | tf_op jit(solution)/shard_map/ppermute | solution.py:18
  18.1 69.7 %all-gather.3.cloned.1.call-done = f32[3,7,256,256]{3,2,0,1:T(8,128)} async-done(((f32[3,7,16,256]{3,2,0,1:T(8,128)}), f32[3,7,256,256]{3,2,0,1:T(8,128)}) %all-gather.3.cloned.1.call-update) | async-done | bytes 5505040 | tf_op jit(solution)/shard_map/all_gather | solution.py:56
  87.8 0.0 copy-start
  87.8 2.0 fusion.7
  89.8 0.0 collective-permute-done
  89.8 1.7 fusion.1
  91.6 1.8 fusion.5
  93.4 1.8 fusion.3
  95.2 0.0 collective-permute-done.1
  95.2 0.0 copy-done.2
  95.2 0.0 copy-done
  95.2 0.6 fusion.9
  95.8 0.6 fusion.11
  96.5 0.6 fusion.13
  97.2 0.1 broadcast_multiply_fusion.1
  97.3 0.0 collective-permute-start.2
  97.3 3.5 %collective-permute-start.3 = (f32[3,7,16,256]{3,2,0,1:T(8,128)S(1)}, f32[3,7,16,256]{3,2,0,1:T(8,128)S(1)}, u32[]{:S(2)}, u32[]{:S(2)}) collective-permute-start(f32[3,7,16,256]{3,2,0,1:T(8,128)S(1)} %broadcast_multiply_fusion.1), channel_id=1, source_target_pairs={{16,0},{32,16},{48,32},{64,48},{80,64},{96,80},{112,96},{128,112},... | collective-permute-start | bytes 1032200 | tf_op jit(solution)/shard_map/ppermute | solution.py:18
  100.8 0.6 fusion.6
  101.4 4.3 %collective-permute-done.2 = f32[3,7,16,256]{3,2,0,1:T(8,128)S(1)} collective-permute-done((f32[3,7,16,256]{3,2,0,1:T(8,128)S(1)}, f32[3,7,16,256]{3,2,0,1:T(8,128)S(1)}, u32[]{:S(2)}, u32[]{:S(2)}) %collective-permute-start.2) | collective-permute-done | bytes 344096 | tf_op jit(solution)/shard_map/ppermute | solution.py:16
  105.7 0.6 fusion
  106.3 0.6 fusion.4
  106.9 0.6 fusion.2
  107.5 0.0 collective-permute-done.3
  107.5 0.6 fusion.8
  108.1 0.6 fusion.10
  108.8 0.6 fusion.12
  109.5 0.9 multiply_subtract_fusion.1
  110.3 0.0 copy-start.3
  110.4 0.0 all-gather.5.cloned.1.call-update
  110.4 0.0 collective-permute-start.4
  110.4 2.9 %collective-permute-start.5 = (f32[3,7,16,256]{3,2,0,1:T(8,128)}, f32[3,7,16,256]{3,2,0,1:T(8,128)S(1)}, u32[]{:S(2)}, u32[]{:S(2)}) collective-permute-start(f32[3,7,16,256]{3,2,0,1:T(8,128)} %multiply_subtract_fusion.1), channel_id=1, source_target_pairs={{16,0},{32,16},{48,32},{64,48},{80,64},{96,80},{112,96},{128,112},... | collective-permute-start | bytes 1032200 | tf_op jit(solution)/shard_map/ppermute | solution.py:18
  113.3 69.4 %all-gather.5.cloned.1.call-done = f32[3,7,256,256]{3,2,0,1:T(8,128)} async-done(((f32[3,7,16,256]{3,2,0,1:T(8,128)}), f32[3,7,256,256]{3,2,0,1:T(8,128)}) %all-gather.5.cloned.1.call-update) | async-done | bytes 5505040 | tf_op jit(solution)/shard_map/all_gather | solution.py:56
  182.8 2.0 fusion.21
  184.7 0.0 collective-permute-done.4
  184.7 1.7 fusion.15
  186.5 1.8 fusion.19
  188.3 1.8 fusion.17
  190.1 0.0 collective-permute-done.5
  190.1 0.0 copy-done.3
  190.1 0.0 copy-done.1
  190.1 0.6 fusion.23
  190.8 0.6 fusion.25
  191.4 0.6 fusion.27
  192.1 0.1 broadcast_multiply_fusion
  192.2 0.0 collective-permute-start.6
  192.2 3.5 %collective-permute-start.7 = (f32[3,7,16,256]{3,2,0,1:T(8,128)S(1)}, f32[3,7,16,256]{3,2,0,1:T(8,128)S(1)}, u32[]{:S(2)}, u32[]{:S(2)}) collective-permute-start(f32[3,7,16,256]{3,2,0,1:T(8,128)S(1)} %broadcast_multiply_fusion), channel_id=1, source_target_pairs={{16,0},{32,16},{48,32},{64,48},{80,64},{96,80},{112,96},{128,112},... | collective-permute-start | bytes 1032200 | tf_op jit(solution)/shard_map/ppermute | solution.py:18
  195.7 0.8 fusion.20
  196.5 4.1 %collective-permute-done.6 = f32[3,7,16,256]{3,2,0,1:T(8,128)S(1)} collective-permute-done((f32[3,7,16,256]{3,2,0,1:T(8,128)S(1)}, f32[3,7,16,256]{3,2,0,1:T(8,128)S(1)}, u32[]{:S(2)}, u32[]{:S(2)}) %collective-permute-start.6) | collective-permute-done | bytes 344096 | tf_op jit(solution)/shard_map/ppermute | solution.py:16
  200.6 0.6 fusion.14
  201.2 0.6 fusion.18
  201.8 0.6 fusion.16
  202.4 0.0 collective-permute-done.7
  202.5 0.6 fusion.22
  203.1 0.6 fusion.24
  203.7 0.6 fusion.26
  204.4 0.1 multiply_subtract_fusion
  204.5 0.8 copy.180
  (30 shorter events, 0.6 us)
Async XLA Ops:
  6.5 81.3 %all-gather.3.cloned.1.call-start = ((), (), s32[]{:S(2)}) async-start(), calls=%async_computation | async-start | bytes 5849088 | tf_op jit(solution)/shard_map/all_gather | solution.py:56
  9.1 86.1 %copy-start.2 = (f32[3,7,16,256]{3,2,0,1:T(8,128)S(1)}, f32[3,7,16,256]{3,2,0,1:T(8,128)}, u32[]{:S(2)}) copy-start(f32[3,7,16,256]{3,2,0,1:T(8,128)} %copy_multiply_fusion) | copy-start | bytes 1032196
  9.1 173.7 %all-gather.5.cloned.1.call-start = ((), (), s32[]{:S(2)}) async-start(), calls=%async_computation.1 | async-start | bytes 5849088 | tf_op jit(solution)/shard_map/all_gather | solution.py:56
  9.1 80.7 %collective-permute-start = (f32[3,7,16,256]{3,2,0,1:T(8,128)}, f32[3,7,16,256]{3,2,0,1:T(8,128)S(1)}, u32[]{:S(2)}, u32[]{:S(2)}) collective-permute-start(f32[3,7,16,256]{3,2,0,1:T(8,128)} %copy_multiply_fusion), channel_id=1, source_target_pairs={{0,16},{16,32},{32,48},{48,64},{64,80},{80,96},{96,112},{112,128},... | collective-permute-start | bytes 1032200 | tf_op jit(solution)/shard_map/ppermute | solution.py:16
  9.2 86.0 %collective-permute-start.1 = (f32[3,7,16,256]{3,2,0,1:T(8,128)}, f32[3,7,16,256]{3,2,0,1:T(8,128)S(1)}, u32[]{:S(2)}, u32[]{:S(2)}) collective-permute-start(f32[3,7,16,256]{3,2,0,1:T(8,128)} %copy_multiply_fusion), channel_id=1, source_target_pairs={{16,0},{32,16},{48,32},{64,48},{80,64},{96,80},{112,96},{128,112},... | collective-permute-start | bytes 1032200 | tf_op jit(solution)/shard_map/ppermute | solution.py:18
  87.8 7.4 %copy-start = (f32[3,7,256,256]{3,2,0,1:T(8,128)S(1)}, f32[3,7,256,256]{3,2,0,1:T(8,128)}, u32[]{:S(2)}) copy-start(f32[3,7,256,256]{3,2,0,1:T(8,128)} %all-gather.3.cloned.1.call-done) | copy-start | bytes 16515076
  97.3 8.4 %collective-permute-start.2 = (f32[3,7,16,256]{3,2,0,1:T(8,128)S(1)}, f32[3,7,16,256]{3,2,0,1:T(8,128)S(1)}, u32[]{:S(2)}, u32[]{:S(2)}) collective-permute-start(f32[3,7,16,256]{3,2,0,1:T(8,128)S(1)} %broadcast_multiply_fusion.1), channel_id=1, source_target_pairs={{0,16},{16,32},{32,48},{48,64},{64,80},{80,96},{96,112},{112,128},... | collective-permute-start | bytes 1032200 | tf_op jit(solution)/shard_map/ppermute | solution.py:16
  97.3 10.2 %collective-permute-start.3 = (f32[3,7,16,256]{3,2,0,1:T(8,128)S(1)}, f32[3,7,16,256]{3,2,0,1:T(8,128)S(1)}, u32[]{:S(2)}, u32[]{:S(2)}) collective-permute-start(f32[3,7,16,256]{3,2,0,1:T(8,128)S(1)} %broadcast_multiply_fusion.1), channel_id=1, source_target_pairs={{16,0},{32,16},{48,32},{64,48},{80,64},{96,80},{112,96},{128,112},... | collective-permute-start | bytes 1032200 | tf_op jit(solution)/shard_map/ppermute | solution.py:18
  110.3 79.8 %copy-start.3 = (f32[3,7,16,256]{3,2,0,1:T(8,128)S(1)}, f32[3,7,16,256]{3,2,0,1:T(8,128)}, u32[]{:S(2)}) copy-start(f32[3,7,16,256]{3,2,0,1:T(8,128)} %multiply_subtract_fusion.1) | copy-start | bytes 1032196
  110.4 74.4 %collective-permute-start.4 = (f32[3,7,16,256]{3,2,0,1:T(8,128)}, f32[3,7,16,256]{3,2,0,1:T(8,128)S(1)}, u32[]{:S(2)}, u32[]{:S(2)}) collective-permute-start(f32[3,7,16,256]{3,2,0,1:T(8,128)} %multiply_subtract_fusion.1), channel_id=1, source_target_pairs={{0,16},{16,32},{32,48},{48,64},{64,80},{80,96},{96,112},{112,128},... | collective-permute-start | bytes 1032200 | tf_op jit(solution)/shard_map/ppermute | solution.py:16
  110.4 79.7 %collective-permute-start.5 = (f32[3,7,16,256]{3,2,0,1:T(8,128)}, f32[3,7,16,256]{3,2,0,1:T(8,128)S(1)}, u32[]{:S(2)}, u32[]{:S(2)}) collective-permute-start(f32[3,7,16,256]{3,2,0,1:T(8,128)} %multiply_subtract_fusion.1), channel_id=1, source_target_pairs={{16,0},{32,16},{48,32},{64,48},{80,64},{96,80},{112,96},{128,112},... | collective-permute-start | bytes 1032200 | tf_op jit(solution)/shard_map/ppermute | solution.py:18
  182.8 7.4 %copy-start.1 = (f32[3,7,256,256]{3,2,0,1:T(8,128)S(1)}, f32[3,7,256,256]{3,2,0,1:T(8,128)}, u32[]{:S(2)}) copy-start(f32[3,7,256,256]{3,2,0,1:T(8,128)} %all-gather.5.cloned.1.call-done) | copy-start | bytes 16515076
  192.2 8.4 %collective-permute-start.6 = (f32[3,7,16,256]{3,2,0,1:T(8,128)S(1)}, f32[3,7,16,256]{3,2,0,1:T(8,128)S(1)}, u32[]{:S(2)}, u32[]{:S(2)}) collective-permute-start(f32[3,7,16,256]{3,2,0,1:T(8,128)S(1)} %broadcast_multiply_fusion), channel_id=1, source_target_pairs={{0,16},{16,32},{32,48},{48,64},{64,80},{80,96},{96,112},{112,128},... | collective-permute-start | bytes 1032200 | tf_op jit(solution)/shard_map/ppermute | solution.py:16
  192.2 10.2 %collective-permute-start.7 = (f32[3,7,16,256]{3,2,0,1:T(8,128)S(1)}, f32[3,7,16,256]{3,2,0,1:T(8,128)S(1)}, u32[]{:S(2)}, u32[]{:S(2)}) collective-permute-start(f32[3,7,16,256]{3,2,0,1:T(8,128)S(1)} %broadcast_multiply_fusion), channel_id=1, source_target_pairs={{16,0},{32,16},{48,32},{64,48},{80,64},{96,80},{112,96},{128,112},... | collective-permute-start | bytes 1032200 | tf_op jit(solution)/shard_map/ppermute | solution.py:18
Sparse Core Ops, SparseCore 0:
  10.4 77.4 all-gather.2
  110.5 72.2 all-gather.4
where the time goes:
time: 212 us
  waiting for transfers between devices  148 us (70%)
  matrix products  26.7 us (13%)
  starting transfers between devices  19 us (9%)
  between operations  13.8 us (7%)
  other arithmetic  4.26 us (2%)
    all_gather x2, waiting for transfers between devices, on_device(): gathered = lax.all_gather(current, 'col', axis=2, tiled=True)  139 us
    dot_general x28, matrix products, contract(): jnp.einsum('ibcs,isr->ibcr', extended[inner_band:inner_band + local_rows,...  26.7 us
    ppermute x4, starting transfers between devices, padded(): lax.ppermute(head, axis, [((i + 1) % count, i) for i in range(count)])  18.9 us
    ppermute x4, waiting for transfers between devices, padded(): lax.ppermute(tail, axis, [(i, (i + 1) % count) for i in range(count)])  8.44 us
  transfers between devices with their start and end apart: 10, of which 4 were waited for; matrix products, arithmetic and copies ran while one was open for 9% of the time, Pallas kernels for 0%

commit v1 on v0

--- a/solution.py
+++ b/solution.py
@@ -53,7 +53,9 @@
     pattern = (offsets[None, :] <= band_widths[:, None]).astype(jnp.float32)[:, :, None, None]
     current = density * pattern
     for purify_step in range(2):
-        gathered = lax.all_gather(current, "col", axis=2, tiled=True)
+        gathered = jnp.concatenate(
+            lax.all_to_all(jnp.stack([current] * lax.axis_size("col")), "col", 0, 0), axis=2
+        )
         square = contract(extend(current), gathered) * pattern
         third_power = contract(extend(square), gathered) * pattern
         current = 3.0 * square - 2.0 * third_power

time: 212 us -> 225 us (1.061)
  the two profiles are of different devices: /device:TPU:2 before, /device:TPU:97 now
where the time goes in v1:
time: 225 us; the launch traced here: 224 us
  waiting for transfers between devices  167 us (74%)
  starting transfers between devices  24.1 us (11%)
  matrix products  16.7 us (7%)
  local copies, waits for them, and re-layouts  12.7 us (6%)
  other arithmetic  3.52 us (2%)
    all_to_all x2, waiting for transfers between devices, on_device(): lax.all_to_all(jnp.stack([current] * lax.axis_size('col')), 'col', 0, 0)  156 us
    dot_general x28, matrix products, contract(): jnp.einsum('ibcs,isr->ibcr', extended[inner_band:inner_band + local_rows,...  16.7 us
    ppermute x4, starting transfers between devices, padded(): lax.ppermute(tail, axis, [(i, (i + 1) % count) for i in range(count)])  12.1 us
    all_to_all x2, starting transfers between devices, on_device(): lax.all_to_all(jnp.stack([current] * lax.axis_size('col')), 'col', 0, 0)  12 us
    ppermute x4, waiting for transfers between devices, padded(): lax.ppermute(tail, axis, [(i, (i + 1) % count) for i in range(count)])  7.19 us
    reshape x2, local copies, waits for them, and re-layouts, on_device(): jnp.concatenate(lax.all_to_all(jnp.stack([current] * lax.axis_size('col')...  6.36 us
    another operation x2, local copies, waits for them, and re-layouts, on_device(): jnp.stack([current] * lax.axis_size('col'))  6.34 us
  transfers between devices with their start and end apart: 10, of which 6 were waited for; matrix products, arithmetic and copies ran while one was open for 7% of the time, Pallas kernels for 0%

profile of v1, /device:TPU:97, one launch (start us, length us, event | category | flops | bytes accessed | tf_op | source)
XLA Modules:
  0.0 224.5 jit_solution(3045528233840822259)
XLA Ops:
  0.0 0.7 compare_convert_fusion
  0.7 1.1 broadcast_multiply_fusion.2
  1.8 3.2 %stack.12 = f32[16,3,7,16,256]{4,3,1,2,0:T(8,128)} broadcast(f32[3,7,16,256]{3,2,0,1:T(8,128)S(1)} %copy.5), dimensions={1,2,3,4} | broadcast | bytes 5849088 | tf_op jit(solution)/shard_map/stack | solution.py:57
  5.0 6.8 %all-to-all-start = ((f32[16,3,7,16,256]{4,3,1,2,0:T(8,128)}), f32[16,3,7,16,256]{4,3,1,2,0:T(8,128)}, u32[]{:S(2)}, u32[]{:S(2)}) async-start(f32[16,3,7,16,256]{4,3,1,2,0:T(8,128)} %stack.12), calls=%async_computation | async-start | bytes 11010048 | tf_op jit(solution)/shard_map/all_to_all | solution.py:57
  11.8 3.7 %collective-permute-start = (f32[3,7,16,256]{3,2,1,0:T(8,128)S(1)}, f32[3,7,16,256]{3,2,1,0:T(8,128)S(1)}, u32[]{:S(2)}, u32[]{:S(2)}) collective-permute-start(f32[3,7,16,256]{3,2,1,0:T(8,128)S(1)} %broadcast_multiply_fusion.2), channel_id=1, source_target_pairs={{0,16},{16,32},{32,48},{48,64},{64,80},{80,96},{96,112},{112,128},... | collective-permute-start | bytes 1032200 | tf_op jit(solution)/shard_map/ppermute | solution.py:16
  15.5 0.0 collective-permute-start.1
  15.5 77.4 %all-to-all-done = f32[16,3,7,16,256]{4,3,1,2,0:T(8,128)} async-done(((f32[16,3,7,16,256]{4,3,1,2,0:T(8,128)}), f32[16,3,7,16,256]{4,3,1,2,0:T(8,128)}, u32[]{:S(2)}, u32[]{:S(2)}) %all-to-all-start) | async-done | bytes 5505056 | tf_op jit(solution)/shard_map/all_to_all | solution.py:57
  92.9 3.2 %copy.6 = f32[3,7,16,16,256]{4,3,2,0,1:T(8,128)S(1)} copy(f32[3,7,16,16,256]{4,3,0,1,2:T(8,128)} %bitcast) | data formatting | bytes 11010048 | tf_op jit(solution)/shard_map/reshape | solution.py:56
  96.1 0.6 fusion.7
  96.7 0.0 collective-permute-done
  96.7 0.6 fusion.5
  97.3 0.6 fusion.1
  97.9 0.6 fusion.3
  98.5 0.0 collective-permute-done.1
  98.5 0.6 fusion.9
  99.1 0.6 fusion.11
  99.8 0.6 fusion.13
  100.5 0.1 broadcast_multiply_fusion.1
  100.6 4.6 %collective-permute-start.2 = (f32[3,7,16,256]{3,2,1,0:T(8,128)S(1)}, f32[3,7,16,256]{3,2,1,0:T(8,128)S(1)}, u32[]{:S(2)}, u32[]{:S(2)}) collective-permute-start(f32[3,7,16,256]{3,2,1,0:T(8,128)S(1)} %broadcast_multiply_fusion.1), channel_id=1, source_target_pairs={{0,16},{16,32},{32,48},{48,64},{64,80},{80,96},{96,112},{112,128},... | collective-permute-start | bytes 1032200 | tf_op jit(solution)/shard_map/ppermute | solution.py:16
  105.1 0.0 collective-permute-start.3
  105.1 0.6 fusion.6
  105.7 3.6 %collective-permute-done.2 = f32[3,7,16,256]{3,2,1,0:T(8,128)S(1)} collective-permute-done((f32[3,7,16,256]{3,2,1,0:T(8,128)S(1)}, f32[3,7,16,256]{3,2,1,0:T(8,128)S(1)}, u32[]{:S(2)}, u32[]{:S(2)}) %collective-permute-start.2) | collective-permute-done | bytes 344096 | tf_op jit(solution)/shard_map/ppermute | solution.py:16
  109.3 0.6 fusion
  109.9 0.6 fusion.4
  110.5 0.6 fusion.2
  111.2 1.9 collective-permute-done.3
  113.0 0.6 fusion.8
  113.6 0.6 fusion.10
  114.3 0.6 fusion.12
  115.0 0.1 multiply_subtract_fusion.1
  115.2 3.2 %stack.15 = f32[16,3,7,16,256]{4,3,1,2,0:T(8,128)} broadcast(f32[3,7,16,256]{3,2,0,1:T(8,128)S(1)} %copy.7), dimensions={1,2,3,4} | broadcast | bytes 5849088 | tf_op jit(solution)/shard_map/stack | solution.py:57
  118.3 5.2 %all-to-all-start.1 = ((f32[16,3,7,16,256]{4,3,1,2,0:T(8,128)}), f32[16,3,7,16,256]{4,3,1,2,0:T(8,128)}, u32[]{:S(2)}, u32[]{:S(2)}) async-start(f32[16,3,7,16,256]{4,3,1,2,0:T(8,128)} %stack.15), calls=%async_computation.1 | async-start | bytes 11010048 | tf_op jit(solution)/shard_map/all_to_all | solution.py:57
  123.5 2.1 collective-permute-start.4
  125.7 0.0 collective-permute-start.5
  125.7 78.7 %all-to-all-done.1 = f32[16,3,7,16,256]{4,3,1,2,0:T(8,128)} async-done(((f32[16,3,7,16,256]{4,3,1,2,0:T(8,128)}), f32[16,3,7,16,256]{4,3,1,2,0:T(8,128)}, u32[]{:S(2)}, u32[]{:S(2)}) %all-to-all-start.1) | async-done | bytes 5505056 | tf_op jit(solution)/shard_map/all_to_all | solution.py:57
  204.4 3.2 %copy.8 = f32[3,7,16,16,256]{4,3,2,0,1:T(8,128)S(1)} copy(f32[3,7,16,16,256]{4,3,0,1,2:T(8,128)} %bitcast.30) | data formatting | bytes 11010048 | tf_op jit(solution)/shard_map/reshape | solution.py:56
  207.6 0.6 fusion.21
  208.1 0.0 collective-permute-done.4
  208.2 0.6 fusion.15
  208.8 0.6 fusion.19
  209.4 0.6 fusion.17
  210.0 0.0 collective-permute-done.5
  210.0 0.6 fusion.23
  210.6 0.6 fusion.25
  211.2 0.6 fusion.27
  211.9 0.1 broadcast_multiply_fusion
  212.0 1.7 collective-permute-start.6
  213.8 0.0 collective-permute-start.7
  213.8 0.6 fusion.20
  214.4 3.6 %collective-permute-done.6 = f32[3,7,16,256]{3,2,1,0:T(8,128)S(1)} collective-permute-done((f32[3,7,16,256]{3,2,1,0:T(8,128)S(1)}, f32[3,7,16,256]{3,2,1,0:T(8,128)S(1)}, u32[]{:S(2)}, u32[]{:S(2)}) %collective-permute-start.6) | collective-permute-done | bytes 344096 | tf_op jit(solution)/shard_map/ppermute | solution.py:16
  218.0 0.6 fusion.14
  218.6 0.6 fusion.18
  219.2 0.6 fusion.16
  219.8 1.9 collective-permute-done.7
  221.6 0.6 fusion.22
  222.3 0.6 fusion.24
  222.9 0.6 fusion.26
  223.6 0.9 multiply_subtract_fusion
  (31 shorter events, 0.6 us)
Async XLA Ops:
  5.0 87.9 %all-to-all-start = ((f32[16,3,7,16,256]{4,3,1,2,0:T(8,128)}), f32[16,3,7,16,256]{4,3,1,2,0:T(8,128)}, u32[]{:S(2)}, u32[]{:S(2)}) async-start(f32[16,3,7,16,256]{4,3,1,2,0:T(8,128)} %stack.12), calls=%async_computation | async-start | bytes 11010048 | tf_op jit(solution)/shard_map/all_to_all | solution.py:57
  11.8 84.9 %collective-permute-start = (f32[3,7,16,256]{3,2,1,0:T(8,128)S(1)}, f32[3,7,16,256]{3,2,1,0:T(8,128)S(1)}, u32[]{:S(2)}, u32[]{:S(2)}) collective-permute-start(f32[3,7,16,256]{3,2,1,0:T(8,128)S(1)} %broadcast_multiply_fusion.2), channel_id=1, source_target_pairs={{0,16},{16,32},{32,48},{48,64},{64,80},{80,96},{96,112},{112,128},... | collective-permute-start | bytes 1032200 | tf_op jit(solution)/shard_map/ppermute | solution.py:16
  15.5 83.0 %collective-permute-start.1 = (f32[3,7,16,256]{3,2,1,0:T(8,128)S(1)}, f32[3,7,16,256]{3,2,1,0:T(8,128)S(1)}, u32[]{:S(2)}, u32[]{:S(2)}) collective-permute-start(f32[3,7,16,256]{3,2,1,0:T(8,128)S(1)} %broadcast_multiply_fusion.2), channel_id=1, source_target_pairs={{16,0},{32,16},{48,32},{64,48},{80,64},{96,80},{112,96},{128,112},... | collective-permute-start | bytes 1032200 | tf_op jit(solution)/shard_map/ppermute | solution.py:18
  100.6 8.8 %collective-permute-start.2 = (f32[3,7,16,256]{3,2,1,0:T(8,128)S(1)}, f32[3,7,16,256]{3,2,1,0:T(8,128)S(1)}, u32[]{:S(2)}, u32[]{:S(2)}) collective-permute-start(f32[3,7,16,256]{3,2,1,0:T(8,128)S(1)} %broadcast_multiply_fusion.1), channel_id=1, source_target_pairs={{0,16},{16,32},{32,48},{48,64},{64,80},{80,96},{96,112},{112,128},... | collective-permute-start | bytes 1032200 | tf_op jit(solution)/shard_map/ppermute | solution.py:16
  105.1 7.9 %collective-permute-start.3 = (f32[3,7,16,256]{3,2,1,0:T(8,128)S(1)}, f32[3,7,16,256]{3,2,1,0:T(8,128)S(1)}, u32[]{:S(2)}, u32[]{:S(2)}) collective-permute-start(f32[3,7,16,256]{3,2,1,0:T(8,128)S(1)} %broadcast_multiply_fusion.1), channel_id=1, source_target_pairs={{16,0},{32,16},{48,32},{64,48},{80,64},{96,80},{112,96},{128,112},... | collective-permute-start | bytes 1032200 | tf_op jit(solution)/shard_map/ppermute | solution.py:18
  118.3 86.0 %all-to-all-start.1 = ((f32[16,3,7,16,256]{4,3,1,2,0:T(8,128)}), f32[16,3,7,16,256]{4,3,1,2,0:T(8,128)}, u32[]{:S(2)}, u32[]{:S(2)}) async-start(f32[16,3,7,16,256]{4,3,1,2,0:T(8,128)} %stack.15), calls=%async_computation.1 | async-start | bytes 11010048 | tf_op jit(solution)/shard_map/all_to_all | solution.py:57
  123.5 84.6 %collective-permute-start.4 = (f32[3,7,16,256]{3,2,1,0:T(8,128)S(1)}, f32[3,7,16,256]{3,2,1,0:T(8,128)S(1)}, u32[]{:S(2)}, u32[]{:S(2)}) collective-permute-start(f32[3,7,16,256]{3,2,1,0:T(8,128)S(1)} %multiply_subtract_fusion.1), channel_id=1, source_target_pairs={{0,16},{16,32},{32,48},{48,64},{64,80},{80,96},{96,112},{112,128},... | collective-permute-start | bytes 1032200 | tf_op jit(solution)/shard_map/ppermute | solution.py:16
  125.7 84.3 %collective-permute-start.5 = (f32[3,7,16,256]{3,2,1,0:T(8,128)S(1)}, f32[3,7,16,256]{3,2,1,0:T(8,128)S(1)}, u32[]{:S(2)}, u32[]{:S(2)}) collective-permute-start(f32[3,7,16,256]{3,2,1,0:T(8,128)S(1)} %multiply_subtract_fusion.1), channel_id=1, source_target_pairs={{16,0},{32,16},{48,32},{64,48},{80,64},{96,80},{112,96},{128,112},... | collective-permute-start | bytes 1032200 | tf_op jit(solution)/shard_map/ppermute | solution.py:18
  212.0 5.9 %collective-permute-start.6 = (f32[3,7,16,256]{3,2,1,0:T(8,128)S(1)}, f32[3,7,16,256]{3,2,1,0:T(8,128)S(1)}, u32[]{:S(2)}, u32[]{:S(2)}) collective-permute-start(f32[3,7,16,256]{3,2,1,0:T(8,128)S(1)} %broadcast_multiply_fusion), channel_id=1, source_target_pairs={{0,16},{16,32},{32,48},{48,64},{64,80},{80,96},{96,112},{112,128},... | collective-permute-start | bytes 1032200 | tf_op jit(solution)/shard_map/ppermute | solution.py:16
  213.8 7.9 %collective-permute-start.7 = (f32[3,7,16,256]{3,2,1,0:T(8,128)S(1)}, f32[3,7,16,256]{3,2,1,0:T(8,128)S(1)}, u32[]{:S(2)}, u32[]{:S(2)}) collective-permute-start(f32[3,7,16,256]{3,2,1,0:T(8,128)S(1)} %broadcast_multiply_fusion), channel_id=1, source_target_pairs={{16,0},{32,16},{48,32},{64,48},{80,64},{96,80},{112,96},{128,112},... | collective-permute-start | bytes 1032200 | tf_op jit(solution)/shard_map/ppermute | solution.py:18
